TPU v7x, 256 devices: a whole 4x4x8 slice. The times are simulated.
256 devices in a mesh: scene: 16 (over y, z_hi), seq: 16 (over z_lo, x, core).
Axes of the slice: x: 4, y: 4, z: 8 (z_hi: 4, z_lo: 2; z = z_hi * 2 + z_lo), core: 2. Of those that a mesh axis runs over, the one named last changes fastest.
Arguments:
- scene_x: bfloat16 [16, 65536, 256], P('scene', 'seq'), may hold values from -6 to 6
- cotangent: bfloat16 [16, 65536, 256], P('scene', 'seq'), may hold values from -6 to 6
- gate_gain: float32 [256], replicated, may hold values from 0.3 to 3
- kernel: bfloat16 [256, 256, 256], P(None, 'seq'), may hold values from -6 to 6
- block_mix: bfloat16 [256, 256], replicated, may hold values from -0.375 to 0.375
- across_mix: bfloat16 [256, 256], replicated, may hold values from -0.375 to 0.375
- across_unmix: bfloat16 [256, 256], replicated, may hold values from -0.375 to 0.375
- block_unmix: bfloat16 [256, 256], replicated, may hold values from -0.375 to 0.375
Outputs:
- mixed: bfloat16 [16, 65536, 256], P('scene', 'seq')
- grad_x: bfloat16 [16, 65536, 256], P('scene', 'seq')
- grad_kernel: float32 [256, 256, 256], P('scene', 'seq')
- grad_gain: float32 [256], replicated
All inputs are finite; a program needn't handle non-finite values.
Results may differ from a plain program's by a relative error of at most 0.007.
Values may be sent and summed in bfloat16 or wider, within the bound.
No kernel may reach another device: no remote copies, remote signals or barrier semaphores. Data moves between devices by JAX's collectives and lax.ppermute only.
A program may use at most 128 MiB of HBM per device.

v0:
```python
import jax
import jax.numpy as jnp
from jax import lax
from jax.sharding import PartitionSpec as P


def on_device(
    scene_x, cotangent, gate_gain, kernel, block_mix, across_mix, across_unmix, block_unmix
):
    f32 = jnp.float32
    bf16 = jnp.bfloat16
    scenes_here, row_count, channels = scene_x.shape
    block_len = block_mix.shape[0]
    local_a = row_count // block_len
    kernel_f = kernel.astype(f32)
    inputs = scene_x.reshape(scenes_here, local_a, block_len, channels)
    first_mix = jnp.einsum("jb,sabc->sajc", block_mix, inputs, preferred_element_type=f32).astype(
        bf16
    )
    spread_mix = lax.all_to_all(first_mix, "seq", split_axis=2, concat_axis=1, tiled=True)
    second_mix = jnp.einsum(
        "ia,sajc->sijc", across_mix, spread_mix, preferred_element_type=f32
    ).astype(bf16)
    weighted = (second_mix.astype(f32) * kernel_f).astype(bf16)
    unmixed = jnp.einsum(
        "pi,sijc->spjc", across_unmix, weighted, preferred_element_type=f32
    ).astype(bf16)
    returned = lax.all_to_all(unmixed, "seq", split_axis=1, concat_axis=2, tiled=True)
    values = jnp.einsum("qj,spjc->spqc", block_unmix, returned, preferred_element_type=f32)
    gate_pre = inputs.astype(f32) * gate_gain
    gate_sig = jax.nn.sigmoid(gate_pre)
    mixed_out = (
        (values * gate_pre * gate_sig).astype(bf16).reshape(scenes_here, row_count, channels)
    )
    upstream = cotangent.reshape(scenes_here, local_a, block_len, channels).astype(f32)
    grad_values = (upstream * gate_pre * gate_sig).astype(bf16)
    grad_gate = upstream * values * gate_sig * (1.0 + gate_pre * (1.0 - gate_sig))
    grad_unmixed = jnp.einsum(
        "qj,spqc->spjc", block_unmix, grad_values, preferred_element_type=f32
    ).astype(bf16)
    spread_grad = lax.all_to_all(grad_unmixed, "seq", split_axis=2, concat_axis=1, tiled=True)
    grad_weighted = jnp.einsum(
        "pi,spjc->sijc", across_unmix, spread_grad, preferred_element_type=f32
    )
    kernel_term = jnp.sum(grad_weighted * second_mix.astype(f32), axis=0)
    kernel_grad = lax.psum_scatter(kernel_term, "scene", scatter_dimension=0, tiled=True)
    grad_second = (grad_weighted * kernel_f).astype(bf16)
    grad_first = jnp.einsum(
        "ia,sijc->sajc", across_mix, grad_second, preferred_element_type=f32
    ).astype(bf16)
    grad_back = lax.all_to_all(grad_first, "seq", split_axis=1, concat_axis=2, tiled=True)
    grad_input = (
        jnp.einsum("jb,sajc->sabc", block_mix, grad_back, preferred_element_type=f32)
        + grad_gate * gate_gain
    )
    grad_input = grad_input.astype(bf16).reshape(scenes_here, row_count, channels)
    gain_term = jnp.sum(inputs.astype(f32) * grad_gate, axis=(0, 1, 2))
    gain_total = lax.psum(gain_term, ("scene", "seq"))
    total_rows = scenes_here * lax.axis_size("scene") * local_a * lax.axis_size("seq") * block_len
    grad_scale = 1.0 / jnp.sqrt(jnp.float32(total_rows))
    return (mixed_out, grad_input, kernel_grad, gain_total * grad_scale)


def solution(mesh):
    return jax.shard_map(
        on_device,
        mesh=mesh,
        in_specs=(
            P("scene", "seq", None),
            P("scene", "seq", None),
            P(),
            P(None, "seq", None),
            P(),
            P(),
            P(),
            P(),
        ),
        out_specs=(P("scene", "seq", None), P("scene", "seq", None), P("scene", "seq", None), P()),
        check_vma=False,
    )
```

profile of v0, /device:TPU:1, one launch (start us, length us, event | category | flops | bytes accessed | tf_op | source)
XLA Modules:
  0.0 281.6 jit_solution(17763689708020302896)
XLA Ops:
  7.2 2.4 convert_bitcast_fusion.4
  9.6 3.1 %copy.39 = bf16[1,16,256,256]{3,1,0,2:T(8,128)(2,1)} copy(bf16[1,16,256,256]{2,3,1,0:T(8,128)(2,1)S(1)} %convert_bitcast_fusion.4) | data formatting | bytes 4194304 | tf_op jit(solution)/shard_map/convert_element_type | solution.py:17
  12.6 7.5 %all-to-all-start = ((bf16[1,16,256,256]{3,1,0,2:T(8,128)(2,1)}), bf16[1,16,256,256]{3,1,0,2:T(8,128)(2,1)}, u32[]{:S(2)}, u32[]{:S(2)}) async-start(bf16[1,16,256,256]{3,1,0,2:T(8,128)(2,1)} %copy.39), calls=%async_computation | async-start | bytes 4194304 | tf_op jit(solution)/shard_map/all_to_all | solution.py:20
  22.5 3.9 %convert_element_type.152 = f32[1,4096,256]{2,1,0:T(8,128)} convert(bf16[1,4096,256]{2,1,0:T(8,128)(2,1)} %param.9) | non-fusion elementwise | flops 1048576 | bytes 6291456 | tf_op jit(solution)/shard_map/convert_element_type | solution.py:35
  26.4 5.5 %copy.47 = f32[16,256,256]{1,2,0:T(8,128)} copy(f32[16,256,256]{2,1,0:T(8,128)} %bitcast.143) | data formatting | bytes 8388608 | tf_op jit(solution)/shard_map/convert_element_type | solution.py:35
  32.0 4.9 %convert_bitcast_fusion.2 = bf16[1,16,256,256]{2,3,1,0:T(8,128)(2,1)} fusion(f32[16,256,256]{1,2,0:T(8,128)} %copy.47, bf16[16,256,256]{1,2,0:T(8,128)(2,1)S(1)} %copy-done.10, f32[256]{0:T(256)S(1)} %copy-done.14, bf16[256,256]{1,0:T(8,128)(2,1)S(1)} %copy-done), kind=kOutput, calls=%fused_computation.37 | convolution fusion | flops 546308096 | bytes 8520704 | tf_op jit(solution)/shard_map/qj,spqc->spjc/dot_general | solution.py:38
  36.9 4.6 %copy.48 = bf16[1,16,256,256]{3,1,0,2:T(8,128)(2,1)} copy(bf16[1,16,256,256]{2,3,1,0:T(8,128)(2,1)} %convert_bitcast_fusion.2) | data formatting | bytes 4194304 | tf_op jit(solution)/shard_map/convert_element_type | solution.py:40
  41.5 6.5 %all-to-all-done = bf16[1,16,256,256]{3,1,0,2:T(8,128)(2,1)} async-done(((bf16[1,16,256,256]{3,1,0,2:T(8,128)(2,1)}), bf16[1,16,256,256]{3,1,0,2:T(8,128)(2,1)}, u32[]{:S(2)}, u32[]{:S(2)}) %all-to-all-start) | async-done | bytes 2097184 | tf_op jit(solution)/shard_map/all_to_all | solution.py:20
  48.0 6.0 %all-to-all-start.2 = ((bf16[1,16,256,256]{3,1,0,2:T(8,128)(2,1)}), bf16[1,16,256,256]{3,1,0,2:T(8,128)(2,1)}, u32[]{:S(2)}, u32[]{:S(2)}) async-start(bf16[1,16,256,256]{3,1,0,2:T(8,128)(2,1)} %copy.48), calls=%async_computation.2 | async-start | bytes 4194304 | tf_op jit(solution)/shard_map/all_to_all | solution.py:41
  54.0 2.7 copy.43
  63.8 4.6 %copy.44 = bf16[1,256,16,256]{3,2,0,1:T(8,128)(2,1)} copy(bf16[1,256,16,256]{1,3,2,0:T(8,128)(2,1)} %convert_bitcast_fusion.3) | data formatting | bytes 4194304 | tf_op jit(solution)/shard_map/convert_element_type | solution.py:27
  68.3 13.4 %all-to-all-done.2 = bf16[1,16,256,256]{3,1,0,2:T(8,128)(2,1)} async-done(((bf16[1,16,256,256]{3,1,0,2:T(8,128)(2,1)}), bf16[1,16,256,256]{3,1,0,2:T(8,128)(2,1)}, u32[]{:S(2)}, u32[]{:S(2)}) %all-to-all-start.2) | async-done | bytes 2097184 | tf_op jit(solution)/shard_map/all_to_all | solution.py:41
  81.7 6.3 %all-to-all-start.1 = ((bf16[1,256,16,256]{3,2,0,1:T(8,128)(2,1)}), bf16[1,256,16,256]{3,2,0,1:T(8,128)(2,1)}, u32[]{:S(2)}, u32[]{:S(2)}) async-start(bf16[1,256,16,256]{3,2,0,1:T(8,128)(2,1)} %copy.44), calls=%async_computation.1 | async-start | bytes 4194304 | tf_op jit(solution)/shard_map/all_to_all | solution.py:28
  94.4 2.5 fusion.15
  96.8 5.5 %copy.55 = f32[256,16,256]{2,1,0:T(8,128)} copy(f32[256,16,256]{0,2,1:T(8,128)} %fusion.15) | data formatting | bytes 8388608 | tf_op jit(solution)/shard_map/reduce_sum | solution.py:45
  103.9 4.2 %convert_bitcast_fusion.1 = bf16[1,256,16,256]{1,3,2,0:T(8,128)(2,1)} fusion(f32[16,256,256]{2,1,0:T(8,128)} %copy-done.1, bf16[256,16,256]{0,2,1:T(8,128)(2,1)S(1)} %copy-done.5, bf16[256,256]{1,0:T(8,128)(2,1)S(1)} %copy-done.11), kind=kOutput, calls=%fused_computation.36 | convolution fusion | flops 541065216 | bytes 8519680 | tf_op jit(solution)/shard_map/ia,sijc->sajc/dot_general | solution.py:48
  108.1 4.5 %copy.52 = bf16[1,256,16,256]{3,2,0,1:T(8,128)(2,1)} copy(bf16[1,256,16,256]{1,3,2,0:T(8,128)(2,1)} %convert_bitcast_fusion.1) | data formatting | bytes 4194304 | tf_op jit(solution)/shard_map/convert_element_type | solution.py:50
  112.6 3.0 %all-to-all-done.1 = bf16[1,256,16,256]{3,2,0,1:T(8,128)(2,1)} async-done(((bf16[1,256,16,256]{3,2,0,1:T(8,128)(2,1)}), bf16[1,256,16,256]{3,2,0,1:T(8,128)(2,1)}, u32[]{:S(2)}, u32[]{:S(2)}) %all-to-all-start.1) | async-done | bytes 2097184 | tf_op jit(solution)/shard_map/all_to_all | solution.py:28
  115.7 6.3 %all-to-all-start.3 = ((bf16[1,256,16,256]{3,2,0,1:T(8,128)(2,1)}), bf16[1,256,16,256]{3,2,0,1:T(8,128)(2,1)S(1)}, u32[]{:S(2)}, u32[]{:S(2)}) async-start(bf16[1,256,16,256]{3,2,0,1:T(8,128)(2,1)} %copy.52), calls=%async_computation.3 | async-start | bytes 4194304 | tf_op jit(solution)/shard_map/all_to_all | solution.py:51
  121.9 3.2 %copy.45 = bf16[1,16,16,16,256]{4,3,2,1,0:T(8,128)(2,1)} copy(bf16[1,16,16,16,256]{4,3,1,2,0:T(8,128)(2,1)} %bitcast.16) | data formatting | bytes 4194304 | tf_op jit(solution)/shard_map/all_to_all | solution.py:28
  125.1 54.0 %all-to-all-done.3 = bf16[1,256,16,256]{3,2,0,1:T(8,128)(2,1)S(1)} async-done(((bf16[1,256,16,256]{3,2,0,1:T(8,128)(2,1)}), bf16[1,256,16,256]{3,2,0,1:T(8,128)(2,1)S(1)}, u32[]{:S(2)}, u32[]{:S(2)}) %all-to-all-start.3) | async-done | bytes 2097184 | tf_op jit(solution)/shard_map/all_to_all | solution.py:51
  183.3 5.0 %fusion.11 = (f32[1,16,256,256]{3,2,1,0:T(8,128)S(1)}, bf16[1,16,256,256]{3,2,1,0:T(8,128)(2,1)}) fusion(f32[1,16,256,256]{3,2,1,0:T(8,128)} %bitcast.144, f32[256]{0:T(256)S(1)} %copy-done.14, bf16[1,4096,256]{2,1,0:T(8,128)(2,1)S(1)} %copy-done.3, bf16[16,256,256]{2,1,0:T(8,128)(2,1)S(1)} %bitcast.152, bf16[256,256]{1,0:T(8,128)(2,1)S(1)} %copy-done), kind=kOutput, calls=%fused_computation.15 | convolution fusion | flops 551550976 | bytes 14812160 | tf_op jit(solution)/shard_map/qj,spjc->spqc/dot_general | solution.py:29
  190.9 78.8 %psum.7 = f32[256]{0:T(256)S(1)} all-reduce(f32[256]{0:T(256)S(1)} %fusion.12), channel_id=1, replica_groups=mesh['scene'=16,'seq'=16] {'scene','seq'}, use_global_device_ids=true, to_apply=%region_2.0 | all-reduce | flops 256 | bytes 2048 | tf_op jit(solution)/shard_map/psum | solution.py:58
  270.3 4.5 %fusion.13 = bf16[1,16,256,256]{3,2,1,0:T(8,128)(2,1)} fusion(f32[1,16,256,256]{3,2,1,0:T(8,128)} %copy-done.6, bf16[16,256,256]{2,1,0:T(8,128)(2,1)S(1)} %bitcast.145, f32[256]{0:T(256)S(1)} %copy-done.14, bf16[256,256]{1,0:T(8,128)(2,1)S(1)} %copy-done.12), kind=kOutput, calls=%fused_computation.18 | convolution fusion | flops 540016640 | bytes 8520704 | tf_op jit(solution)/shard_map/jb,sajc->sabc/dot_general | solution.py:53
  (44 shorter events, 24.7 us)
Async XLA Ops:
  7.2 24.8 %copy-start = (bf16[256,256]{1,0:T(8,128)(2,1)S(1)}, bf16[256,256]{1,0:T(8,128)(2,1)}, u32[]{:S(2)}) copy-start(bf16[256,256]{1,0:T(8,128)(2,1)} %param.15) | copy-start | bytes 393220
  12.6 7.5 %copy-start.2 = (bf16[1,4096,256]{2,1,0:T(8,128)(2,1)S(1)}, bf16[1,4096,256]{2,1,0:T(8,128)(2,1)}, u32[]{:S(2)}) copy-start(bf16[1,4096,256]{2,1,0:T(8,128)(2,1)} %param.8) | copy-start | bytes 6291460
  12.6 35.3 %all-to-all-start = ((bf16[1,16,256,256]{3,1,0,2:T(8,128)(2,1)}), bf16[1,16,256,256]{3,1,0,2:T(8,128)(2,1)}, u32[]{:S(2)}, u32[]{:S(2)}) async-start(bf16[1,16,256,256]{3,1,0,2:T(8,128)(2,1)} %copy.39), calls=%async_computation | async-start | bytes 4194304 | tf_op jit(solution)/shard_map/all_to_all | solution.py:20
  26.4 5.6 %copy-start.10 = (bf16[16,256,256]{1,2,0:T(8,128)(2,1)S(1)}, bf16[16,256,256]{1,2,0:T(8,128)(2,1)}, u32[]{:S(2)}) copy-start(bf16[16,256,256]{1,2,0:T(8,128)(2,1)} %copy.46) | copy-start | bytes 6291460
  26.4 5.6 %copy-start.14 = (f32[256]{0:T(256)S(1)}, f32[256]{0:T(256)}, u32[]{:S(2)}) copy-start(f32[256]{0:T(256)} %param.10) | copy-start | bytes 3076
  41.5 12.5 %copy-start.8 = (bf16[256,16,256]{2,1,0:T(8,128)(2,1)S(1)}, bf16[256,16,256]{2,1,0:T(8,128)(2,1)}, u32[]{:S(2)}) copy-start(bf16[256,16,256]{2,1,0:T(8,128)(2,1)} %param.11) | copy-start | bytes 6291460
  48.0 33.7 %all-to-all-start.2 = ((bf16[1,16,256,256]{3,1,0,2:T(8,128)(2,1)}), bf16[1,16,256,256]{3,1,0,2:T(8,128)(2,1)}, u32[]{:S(2)}, u32[]{:S(2)}) async-start(bf16[1,16,256,256]{3,1,0,2:T(8,128)(2,1)} %copy.48), calls=%async_computation.2 | async-start | bytes 4194304 | tf_op jit(solution)/shard_map/all_to_all | solution.py:41
  59.0 0.9 copy-start.11
  59.9 1.7 copy-start.4
  60.0 1.7 copy-start.13
  81.7 34.0 %all-to-all-start.1 = ((bf16[1,256,16,256]{3,2,0,1:T(8,128)(2,1)}), bf16[1,256,16,256]{3,2,0,1:T(8,128)(2,1)}, u32[]{:S(2)}, u32[]{:S(2)}) async-start(bf16[1,256,16,256]{3,2,0,1:T(8,128)(2,1)} %copy.44), calls=%async_computation.1 | async-start | bytes 4194304 | tf_op jit(solution)/shard_map/all_to_all | solution.py:28
  88.0 186.8 %reduce-scatter.2.cloned.1.call-start = ((), (), s32[]{:S(2)}) async-start(), calls=%async_computation.5 | async-start | bytes 4456448 | tf_op jit(solution)/shard_map/reduce_scatter | solution.py:46
  92.4 2.0 copy-start.1
  102.3 1.6 copy-start.5
  115.7 63.4 %all-to-all-start.3 = ((bf16[1,256,16,256]{3,2,0,1:T(8,128)(2,1)}), bf16[1,256,16,256]{3,2,0,1:T(8,128)(2,1)S(1)}, u32[]{:S(2)}, u32[]{:S(2)}) async-start(bf16[1,256,16,256]{3,2,0,1:T(8,128)(2,1)} %copy.52), calls=%async_computation.3 | async-start | bytes 4194304 | tf_op jit(solution)/shard_map/all_to_all | solution.py:51
  179.1 1.3 copy-start.7
  180.4 2.2 copy-start.3
  180.4 2.9 %copy-start.9 = (bf16[1,16,16,16,256]{4,3,2,1,0:T(8,128)(2,1)S(1)}, bf16[1,16,16,16,256]{4,3,2,1,0:T(8,128)(2,1)}, u32[]{:S(2)}) copy-start(bf16[1,16,16,16,256]{4,3,2,1,0:T(8,128)(2,1)} %copy.45) | copy-start | bytes 6291460
  188.3 2.0 copy-start.6
  190.2 80.1 %copy-start.12 = (bf16[256,256]{1,0:T(8,128)(2,1)S(1)}, bf16[256,256]{1,0:T(8,128)(2,1)}, u32[]{:S(2)}) copy-start(bf16[256,256]{1,0:T(8,128)(2,1)} %param.12) | copy-start | bytes 393220
Sparse Core Ops, SparseCore 0:
  102.5 100.8 reduce-scatter.1
where the time goes:
time: 283 us; the launch traced here: 282 us
  blocking collectives  78.8 us (28%)
  waiting for transfers between devices  76.9 us (27%)
  local copies, waits for them, and re-layouts  51.5 us (18%)
  matrix products  26.4 us (9%)
  starting transfers between devices  26.2 us (9%)
  between operations  14.2 us (5%)
  other arithmetic  7.59 us (3%)
    psum x1, blocking collectives, on_device(): gain_total = lax.psum(gain_term, ('scene', 'seq'))  78.8 us
    all_to_all x1, waiting for transfers between devices, on_device(): lax.all_to_all(grad_first, 'seq', split_axis=1, concat_axis=2, tiled=True)  54 us
    all_to_all x1, waiting for transfers between devices, on_device(): lax.all_to_all(grad_unmixed, 'seq', split_axis=2, concat_axis=1, tiled=True)  13.4 us
    unnamed x31, local copies, waits for them, and re-layouts  11.2 us
    all_to_all x1, starting transfers between devices, on_device(): lax.all_to_all(first_mix, 'seq', split_axis=2, concat_axis=1, tiled=True)  7.5 us
    all_to_all x1, waiting for transfers between devices, on_device(): lax.all_to_all(first_mix, 'seq', split_axis=2, concat_axis=1, tiled=True)  6.49 us
    all_to_all x1, starting transfers between devices, on_device(): lax.all_to_all(grad_first, 'seq', split_axis=1, concat_axis=2, tiled=True)  6.26 us
    all_to_all x1, starting transfers between devices, on_device(): lax.all_to_all(unmixed, 'seq', split_axis=1, concat_axis=2, tiled=True)  6.26 us
  transfers between devices with their start and end apart: 5, of which 4 were waited for; matrix products, arithmetic and copies ran while one was open for 25% of the time, Pallas kernels for 0%

commit v1 on v0

--- a/solution.py
+++ b/solution.py
@@ -55,7 +55,7 @@
     )
     grad_input = grad_input.astype(bf16).reshape(scenes_here, row_count, channels)
     gain_term = jnp.sum(inputs.astype(f32) * grad_gate, axis=(0, 1, 2))
-    gain_total = lax.psum(gain_term, ("scene", "seq"))
+    gain_total = jnp.sum(lax.all_gather(gain_term, axis_name=("scene", "seq")), axis=0)
     total_rows = scenes_here * lax.axis_size("scene") * local_a * lax.axis_size("seq") * block_len
     grad_scale = 1.0 / jnp.sqrt(jnp.float32(total_rows))
     return (mixed_out, grad_input, kernel_grad, gain_total * grad_scale)

time: 283 us -> 268 us (0.947)
  blocking collectives: 78.8 us -> 64.2 us
    psum x1 -> x0, blocking collectives: 78.8 us -> none  [on_device(): gain_total = lax.psum(gain_term, ('scene', 'seq'))]
    all_gather x0 -> x1, blocking collectives: none -> 64.2 us  [on_device(): lax.all_gather(gain_term, axis_name=('scene', 'seq'))]
  transfers between devices with their start and end apart: 5 -> 5, of which waited for: 4 -> 4; matrix products, arithmetic and copies ran while one was open for 25% -> 27% of each run, Pallas kernels for 0% -> 0%
where the time goes in v1:
time: 268 us; the launch traced here: 267 us
  waiting for transfers between devices  76.9 us (29%)
  blocking collectives  64.2 us (24%)
  local copies, waits for them, and re-layouts  50.8 us (19%)
  matrix products  26.4 us (10%)
  starting transfers between devices  26.2 us (10%)
  between operations  14.2 us (5%)
  other arithmetic  7.89 us (3%)
    all_gather x1, blocking collectives, on_device(): lax.all_gather(gain_term, axis_name=('scene', 'seq'))  64.2 us
    all_to_all x1, waiting for transfers between devices, on_device(): lax.all_to_all(grad_first, 'seq', split_axis=1, concat_axis=2, tiled=True)  54 us
    all_to_all x1, waiting for transfers between devices, on_device(): lax.all_to_all(grad_unmixed, 'seq', split_axis=2, concat_axis=1, tiled=True)  13.4 us
    unnamed x31, local copies, waits for them, and re-layouts  10.4 us
    all_to_all x1, starting transfers between devices, on_device(): lax.all_to_all(first_mix, 'seq', split_axis=2, concat_axis=1, tiled=True)  7.5 us
    all_to_all x1, waiting for transfers between devices, on_device(): lax.all_to_all(first_mix, 'seq', split_axis=2, concat_axis=1, tiled=True)  6.49 us
    all_to_all x1, starting transfers between devices, on_device(): lax.all_to_all(grad_first, 'seq', split_axis=1, concat_axis=2, tiled=True)  6.26 us
    all_to_all x1, starting transfers between devices, on_device(): lax.all_to_all(unmixed, 'seq', split_axis=1, concat_axis=2, tiled=True)  6.26 us
  transfers between devices with their start and end apart: 5, of which 4 were waited for; matrix products, arithmetic and copies ran while one was open for 27% of the time, Pallas kernels for 0%

profile of v1, /device:TPU:1, one launch (start us, length us, event | category | flops | bytes accessed | tf_op | source)
XLA Modules:
  0.0 266.6 jit_solution(2077352756767768912)
XLA Ops:
  7.2 2.4 convert_bitcast_fusion.4
  9.6 3.1 %copy.39 = bf16[1,16,256,256]{3,1,0,2:T(8,128)(2,1)} copy(bf16[1,16,256,256]{2,3,1,0:T(8,128)(2,1)S(1)} %convert_bitcast_fusion.4) | data formatting | bytes 4194304 | tf_op jit(solution)/shard_map/convert_element_type | solution.py:17
  12.6 7.5 %all-to-all-start = ((bf16[1,16,256,256]{3,1,0,2:T(8,128)(2,1)}), bf16[1,16,256,256]{3,1,0,2:T(8,128)(2,1)}, u32[]{:S(2)}, u32[]{:S(2)}) async-start(bf16[1,16,256,256]{3,1,0,2:T(8,128)(2,1)} %copy.39), calls=%async_computation | async-start | bytes 4194304 | tf_op jit(solution)/shard_map/all_to_all | solution.py:20
  22.5 3.9 %convert_element_type.152 = f32[1,4096,256]{2,1,0:T(8,128)} convert(bf16[1,4096,256]{2,1,0:T(8,128)(2,1)} %param.9) | non-fusion elementwise | flops 1048576 | bytes 6291456 | tf_op jit(solution)/shard_map/convert_element_type | solution.py:35
  26.4 5.5 %copy.47 = f32[16,256,256]{1,2,0:T(8,128)} copy(f32[16,256,256]{2,1,0:T(8,128)} %bitcast.144) | data formatting | bytes 8388608 | tf_op jit(solution)/shard_map/convert_element_type | solution.py:35
  32.0 4.9 %convert_bitcast_fusion.2 = bf16[1,16,256,256]{2,3,1,0:T(8,128)(2,1)} fusion(f32[16,256,256]{1,2,0:T(8,128)} %copy.47, bf16[16,256,256]{1,2,0:T(8,128)(2,1)S(1)} %copy-done.10, f32[256]{0:T(256)S(1)} %copy-done.14, bf16[256,256]{1,0:T(8,128)(2,1)S(1)} %copy-done), kind=kOutput, calls=%fused_computation.37 | convolution fusion | flops 546308096 | bytes 8520704 | tf_op jit(solution)/shard_map/qj,spqc->spjc/dot_general | solution.py:38
  36.9 4.6 %copy.48 = bf16[1,16,256,256]{3,1,0,2:T(8,128)(2,1)} copy(bf16[1,16,256,256]{2,3,1,0:T(8,128)(2,1)} %convert_bitcast_fusion.2) | data formatting | bytes 4194304 | tf_op jit(solution)/shard_map/convert_element_type | solution.py:40
  41.5 6.5 %all-to-all-done = bf16[1,16,256,256]{3,1,0,2:T(8,128)(2,1)} async-done(((bf16[1,16,256,256]{3,1,0,2:T(8,128)(2,1)}), bf16[1,16,256,256]{3,1,0,2:T(8,128)(2,1)}, u32[]{:S(2)}, u32[]{:S(2)}) %all-to-all-start) | async-done | bytes 2097184 | tf_op jit(solution)/shard_map/all_to_all | solution.py:20
  48.0 6.0 %all-to-all-start.2 = ((bf16[1,16,256,256]{3,1,0,2:T(8,128)(2,1)}), bf16[1,16,256,256]{3,1,0,2:T(8,128)(2,1)}, u32[]{:S(2)}, u32[]{:S(2)}) async-start(bf16[1,16,256,256]{3,1,0,2:T(8,128)(2,1)} %copy.48), calls=%async_computation.2 | async-start | bytes 4194304 | tf_op jit(solution)/shard_map/all_to_all | solution.py:41
  54.0 2.7 %copy.43 = bf16[256,16,256]{0,2,1:T(8,128)(2,1)} copy(bf16[256,16,256]{2,1,0:T(8,128)(2,1)S(1)} %copy-done.8) | data formatting | bytes 4194304 | tf_op args[3]
  63.8 4.6 %copy.44 = bf16[1,256,16,256]{3,2,0,1:T(8,128)(2,1)} copy(bf16[1,256,16,256]{1,3,2,0:T(8,128)(2,1)} %convert_bitcast_fusion.3) | data formatting | bytes 4194304 | tf_op jit(solution)/shard_map/convert_element_type | solution.py:27
  68.3 13.4 %all-to-all-done.2 = bf16[1,16,256,256]{3,1,0,2:T(8,128)(2,1)} async-done(((bf16[1,16,256,256]{3,1,0,2:T(8,128)(2,1)}), bf16[1,16,256,256]{3,1,0,2:T(8,128)(2,1)}, u32[]{:S(2)}, u32[]{:S(2)}) %all-to-all-start.2) | async-done | bytes 2097184 | tf_op jit(solution)/shard_map/all_to_all | solution.py:41
  81.7 6.3 %all-to-all-start.1 = ((bf16[1,256,16,256]{3,2,0,1:T(8,128)(2,1)}), bf16[1,256,16,256]{3,2,0,1:T(8,128)(2,1)}, u32[]{:S(2)}, u32[]{:S(2)}) async-start(bf16[1,256,16,256]{3,2,0,1:T(8,128)(2,1)} %copy.44), calls=%async_computation.1 | async-start | bytes 4194304 | tf_op jit(solution)/shard_map/all_to_all | solution.py:28
  94.4 2.5 fusion.15
  96.8 5.5 %copy.55 = f32[256,16,256]{2,1,0:T(8,128)} copy(f32[256,16,256]{0,2,1:T(8,128)} %fusion.15) | data formatting | bytes 8388608 | tf_op jit(solution)/shard_map/reduce_sum | solution.py:45
  103.9 4.2 %convert_bitcast_fusion.1 = bf16[1,256,16,256]{1,3,2,0:T(8,128)(2,1)} fusion(f32[16,256,256]{2,1,0:T(8,128)} %copy-done.1, bf16[256,16,256]{0,2,1:T(8,128)(2,1)S(1)} %copy-done.5, bf16[256,256]{1,0:T(8,128)(2,1)S(1)} %copy-done.11), kind=kOutput, calls=%fused_computation.36 | convolution fusion | flops 541065216 | bytes 8519680 | tf_op jit(solution)/shard_map/ia,sijc->sajc/dot_general | solution.py:48
  108.1 4.5 %copy.52 = bf16[1,256,16,256]{3,2,0,1:T(8,128)(2,1)} copy(bf16[1,256,16,256]{1,3,2,0:T(8,128)(2,1)} %convert_bitcast_fusion.1) | data formatting | bytes 4194304 | tf_op jit(solution)/shard_map/convert_element_type | solution.py:50
  112.6 3.0 %all-to-all-done.1 = bf16[1,256,16,256]{3,2,0,1:T(8,128)(2,1)} async-done(((bf16[1,256,16,256]{3,2,0,1:T(8,128)(2,1)}), bf16[1,256,16,256]{3,2,0,1:T(8,128)(2,1)}, u32[]{:S(2)}, u32[]{:S(2)}) %all-to-all-start.1) | async-done | bytes 2097184 | tf_op jit(solution)/shard_map/all_to_all | solution.py:28
  115.7 6.3 %all-to-all-start.3 = ((bf16[1,256,16,256]{3,2,0,1:T(8,128)(2,1)}), bf16[1,256,16,256]{3,2,0,1:T(8,128)(2,1)S(1)}, u32[]{:S(2)}, u32[]{:S(2)}) async-start(bf16[1,256,16,256]{3,2,0,1:T(8,128)(2,1)} %copy.52), calls=%async_computation.3 | async-start | bytes 4194304 | tf_op jit(solution)/shard_map/all_to_all | solution.py:51
  121.9 3.2 %copy.45 = bf16[1,16,16,16,256]{4,3,2,1,0:T(8,128)(2,1)} copy(bf16[1,16,16,16,256]{4,3,1,2,0:T(8,128)(2,1)} %bitcast.16) | data formatting | bytes 4194304 | tf_op jit(solution)/shard_map/all_to_all | solution.py:28
  125.1 54.0 %all-to-all-done.3 = bf16[1,256,16,256]{3,2,0,1:T(8,128)(2,1)S(1)} async-done(((bf16[1,256,16,256]{3,2,0,1:T(8,128)(2,1)}), bf16[1,256,16,256]{3,2,0,1:T(8,128)(2,1)S(1)}, u32[]{:S(2)}, u32[]{:S(2)}) %all-to-all-start.3) | async-done | bytes 2097184 | tf_op jit(solution)/shard_map/all_to_all | solution.py:51
  183.3 5.0 %fusion.11 = (f32[1,16,256,256]{3,2,1,0:T(8,128)S(1)}, bf16[1,16,256,256]{3,2,1,0:T(8,128)(2,1)}) fusion(f32[1,16,256,256]{3,2,1,0:T(8,128)} %bitcast.145, f32[256]{0:T(256)S(1)} %copy-done.14, bf16[1,4096,256]{2,1,0:T(8,128)(2,1)S(1)} %copy-done.3, bf16[16,256,256]{2,1,0:T(8,128)(2,1)S(1)} %bitcast.153, bf16[256,256]{1,0:T(8,128)(2,1)S(1)} %copy-done), kind=kOutput, calls=%fused_computation.15 | convolution fusion | flops 551550976 | bytes 14812160 | tf_op jit(solution)/shard_map/qj,spjc->spqc/dot_general | solution.py:29
  190.2 64.2 %all-gather.1 = f32[256,1,256]{2,1,0:T(1,128)S(1)} all-gather(f32[1,1,256]{2,1,0:T(1,128)S(1)} %bitcast.154), channel_id=2, replica_groups=mesh['scene'=16,'seq'=16] {'scene','seq'}, dimensions={0}, use_global_device_ids=true | all-gather | bytes 263168 | tf_op jit(solution)/shard_map/all_gather | solution.py:58
  255.3 4.5 %fusion.13 = bf16[1,16,256,256]{3,2,1,0:T(8,128)(2,1)} fusion(f32[1,16,256,256]{3,2,1,0:T(8,128)} %copy-done.6, bf16[16,256,256]{2,1,0:T(8,128)(2,1)S(1)} %bitcast.146, f32[256]{0:T(256)S(1)} %copy-done.14, bf16[256,256]{1,0:T(8,128)(2,1)S(1)} %copy-done.12), kind=kOutput, calls=%fused_computation.18 | convolution fusion | flops 540016640 | bytes 8520704 | tf_op jit(solution)/shard_map/jb,sajc->sabc/dot_general | solution.py:53
  (45 shorter events, 24.3 us)
Async XLA Ops:
  7.2 24.8 %copy-start = (bf16[256,256]{1,0:T(8,128)(2,1)S(1)}, bf16[256,256]{1,0:T(8,128)(2,1)}, u32[]{:S(2)}) copy-start(bf16[256,256]{1,0:T(8,128)(2,1)} %param.15) | copy-start | bytes 393220
  12.6 7.5 %copy-start.2 = (bf16[1,4096,256]{2,1,0:T(8,128)(2,1)S(1)}, bf16[1,4096,256]{2,1,0:T(8,128)(2,1)}, u32[]{:S(2)}) copy-start(bf16[1,4096,256]{2,1,0:T(8,128)(2,1)} %param.8) | copy-start | bytes 6291460
  12.6 35.3 %all-to-all-start = ((bf16[1,16,256,256]{3,1,0,2:T(8,128)(2,1)}), bf16[1,16,256,256]{3,1,0,2:T(8,128)(2,1)}, u32[]{:S(2)}, u32[]{:S(2)}) async-start(bf16[1,16,256,256]{3,1,0,2:T(8,128)(2,1)} %copy.39), calls=%async_computation | async-start | bytes 4194304 | tf_op jit(solution)/shard_map/all_to_all | solution.py:20
  26.4 5.6 %copy-start.10 = (bf16[16,256,256]{1,2,0:T(8,128)(2,1)S(1)}, bf16[16,256,256]{1,2,0:T(8,128)(2,1)}, u32[]{:S(2)}) copy-start(bf16[16,256,256]{1,2,0:T(8,128)(2,1)} %copy.46) | copy-start | bytes 6291460
  26.4 5.6 %copy-start.14 = (f32[256]{0:T(256)S(1)}, f32[256]{0:T(256)}, u32[]{:S(2)}) copy-start(f32[256]{0:T(256)} %param.10) | copy-start | bytes 3076
  41.5 12.5 %copy-start.8 = (bf16[256,16,256]{2,1,0:T(8,128)(2,1)S(1)}, bf16[256,16,256]{2,1,0:T(8,128)(2,1)}, u32[]{:S(2)}) copy-start(bf16[256,16,256]{2,1,0:T(8,128)(2,1)} %param.11) | copy-start | bytes 6291460
  48.0 33.7 %all-to-all-start.2 = ((bf16[1,16,256,256]{3,1,0,2:T(8,128)(2,1)}), bf16[1,16,256,256]{3,1,0,2:T(8,128)(2,1)}, u32[]{:S(2)}, u32[]{:S(2)}) async-start(bf16[1,16,256,256]{3,1,0,2:T(8,128)(2,1)} %copy.48), calls=%async_computation.2 | async-start | bytes 4194304 | tf_op jit(solution)/shard_map/all_to_all | solution.py:41
  59.0 0.9 copy-start.11
  59.9 1.7 copy-start.4
  60.0 1.7 copy-start.13
  81.7 34.0 %all-to-all-start.1 = ((bf16[1,256,16,256]{3,2,0,1:T(8,128)(2,1)}), bf16[1,256,16,256]{3,2,0,1:T(8,128)(2,1)}, u32[]{:S(2)}, u32[]{:S(2)}) async-start(bf16[1,256,16,256]{3,2,0,1:T(8,128)(2,1)} %copy.44), calls=%async_computation.1 | async-start | bytes 4194304 | tf_op jit(solution)/shard_map/all_to_all | solution.py:28
  88.0 171.8 %reduce-scatter.2.cloned.1.call-start = ((), (), s32[]{:S(2)}) async-start(), calls=%async_computation.5 | async-start | bytes 4456448 | tf_op jit(solution)/shard_map/reduce_scatter | solution.py:46
  92.4 2.0 copy-start.1
  102.3 1.6 copy-start.5
  115.7 63.4 %all-to-all-start.3 = ((bf16[1,256,16,256]{3,2,0,1:T(8,128)(2,1)}), bf16[1,256,16,256]{3,2,0,1:T(8,128)(2,1)S(1)}, u32[]{:S(2)}, u32[]{:S(2)}) async-start(bf16[1,256,16,256]{3,2,0,1:T(8,128)(2,1)} %copy.52), calls=%async_computation.3 | async-start | bytes 4194304 | tf_op jit(solution)/shard_map/all_to_all | solution.py:51
  179.1 1.3 copy-start.7
  180.4 2.2 copy-start.3
  180.4 2.9 %copy-start.9 = (bf16[1,16,16,16,256]{4,3,2,1,0:T(8,128)(2,1)S(1)}, bf16[1,16,16,16,256]{4,3,2,1,0:T(8,128)(2,1)}, u32[]{:S(2)}) copy-start(bf16[1,16,16,16,256]{4,3,2,1,0:T(8,128)(2,1)} %copy.45) | copy-start | bytes 6291460
  188.3 2.0 copy-start.6
  188.3 67.0 %copy-start.12 = (bf16[256,256]{1,0:T(8,128)(2,1)S(1)}, bf16[256,256]{1,0:T(8,128)(2,1)}, u32[]{:S(2)}) copy-start(bf16[256,256]{1,0:T(8,128)(2,1)} %param.12) | copy-start | bytes 393220
Sparse Core Ops, SparseCore 0:
  102.5 100.6 reduce-scatter.1
